TPU v7x, 256 devices: a whole 4x4x8 slice. The times are simulated.
256 devices in a mesh: section: 4 (over y), expert: 64 (over x, z, core).
Axes of the slice: x: 4, y: 4, z: 8, core: 2. Of those that a mesh axis runs over, the one named last changes fastest.
Arguments:
- tokens: bfloat16 [1024, 4096], P('expert', 'section'), may hold values from -6 to 6
- cotangent: bfloat16 [1024, 4096], P('expert', 'section'), may hold values from -6 to 6
- routes: int32 [1024, 2], P('expert'), may hold values from 0 to 7, all different within a row; in each aligned block of 16 rows (0 to 15, 16 to 31, ...) at most 6 rows name the same one
- w_router: bfloat16 [4096, 8], P('section'), may hold values from -0.09375 to 0.09375
- w_gate: bfloat16 [64, 4096, 1024], P('expert', None, 'section'), may hold values from -0.09375 to 0.09375
- w_up: bfloat16 [64, 4096, 1024], P('expert', None, 'section'), may hold values from -0.09375 to 0.09375
- w_down: bfloat16 [64, 1024, 4096], P('expert', 'section'), may hold values from -0.0625 to 0.0625
Outputs:
- mixed: bfloat16 [1024, 4096], P('expert', 'section')
- grad_tokens: bfloat16 [1024, 4096], P('expert', 'section')
- grad_router: float32 [4096, 8], P('section')
- grad_gate: bfloat16 [64, 4096, 1024], P('expert', None, 'section')
- grad_up: bfloat16 [64, 4096, 1024], P('expert', None, 'section')
- grad_down: bfloat16 [64, 1024, 4096], P('expert', 'section')
Inputs may be any that keep to these rules, and one draw needn't show every extreme that they name: `routes`: each token names two different experts. Within each aligned block of 16 tokens no expert is named by more than 6 tokens, and in every draw some block has an expert named by exactly 6 tokens.
All inputs are finite; a program needn't handle non-finite values.
Results may differ from a plain program's by a relative error of at most 0.023.
Values may be sent and summed in bfloat16 or wider, within the bound.
No kernel may reach another device: no remote copies, remote signals or barrier semaphores. Data moves between devices by JAX's collectives and lax.ppermute only.
A program may use at most 128 MiB of HBM per device.

v0:
```python
import jax
import jax.numpy as jnp
import numpy as np
from jax import lax
from jax.sharding import Mesh
from jax.sharding import PartitionSpec as P

CAP = 6
LANES = 128
EXPERT_AXES = ("ex", "ez", "ec")


def expert_size():
    size = 1
    for name in EXPERT_AXES:
        size = size * lax.axis_size(name)
    return size


def per_device(tokens, cotangent, routes, w_router, w_gate, w_up, w_down):
    highest = lax.Precision.HIGHEST
    experts = w_router.shape[1]
    groups = expert_size() // experts
    capacity = CAP
    tok_count, width = tokens.shape
    n_section = lax.axis_size("section")
    slot_total = experts * capacity
    route_hot = routes[:, :, None] == jnp.arange(experts, dtype=jnp.int32)[None, None, :]
    zero_f = jnp.zeros((), jnp.float32)
    counts_flat = route_hot.astype(jnp.int32).reshape(2 * tok_count, experts)
    earlier = jnp.cumsum(counts_flat, axis=0) - counts_flat
    position = jnp.sum(earlier * counts_flat, axis=1).reshape(tok_count, 2)
    slot_row = routes * capacity + position
    slot_ids = jnp.arange(slot_total, dtype=jnp.int32)[None, :]
    pick_first = slot_row[:, 0:1] == slot_ids
    pick_second = slot_row[:, 1:2] == slot_ids
    pick_both = (pick_first | pick_second).astype(jnp.bfloat16)
    x_source = jnp.einsum(
        "ts,td->sd", pick_both, tokens, preferred_element_type=jnp.float32
    ).astype(jnp.bfloat16)
    zero_i = jnp.zeros((), jnp.int32)
    other_slot = jnp.sum(
        jnp.where(pick_first, routes[:, 1:2], zero_i)
        + jnp.where(pick_second, routes[:, 0:1], zero_i),
        axis=0,
    )
    half = capacity * width // LANES
    meta = jnp.zeros((experts, 16, LANES), jnp.bfloat16)
    meta = meta.at[:, 0, :capacity].set(other_slot.reshape(experts, capacity).astype(jnp.bfloat16))

    def spread(block):
        rows = block.shape[1]
        return jnp.broadcast_to(block[:, None], (experts, groups, rows, LANES)).reshape(
            experts * groups, rows, LANES
        )

    x_block = x_source.reshape(experts, half, LANES)
    x_recv = lax.all_to_all(spread(x_block), EXPERT_AXES, 0, 0, tiled=True)
    cot_source = jnp.einsum(
        "ts,td->sd", pick_both, cotangent, preferred_element_type=jnp.float32
    ).astype(jnp.bfloat16)
    c_block = jnp.concatenate([cot_source.reshape(experts, half, LANES), meta], axis=1)
    row_total = x_recv.shape[0] * capacity
    x_recv = x_recv.reshape(row_total, width)
    x_rows = lax.all_gather(x_recv, "section", axis=1, tiled=True)
    c_block, x_recv = lax.optimization_barrier((c_block, x_recv))
    c_recv = lax.all_to_all(spread(c_block), EXPERT_AXES, 0, 0, tiled=True)
    cot_recv = c_recv[:, :half].reshape(row_total, width)
    other_recv = c_recv[:, half, :capacity].astype(jnp.int32).reshape(row_total)
    w_router, x_recv = lax.optimization_barrier((w_router, x_recv))
    partial_logits = jnp.dot(tokens, w_router, preferred_element_type=jnp.float32)
    logits = lax.psum(partial_logits, "section")
    chosen = jnp.sum(jnp.where(route_hot, logits[:, None, :], zero_f), axis=2)
    gate_first = 1.0 / (1.0 + jnp.exp(chosen[:, 1] - chosen[:, 0]))
    gate_second = 1.0 / (1.0 + jnp.exp(chosen[:, 0] - chosen[:, 1]))
    cot_float = cotangent.astype(jnp.float32)
    row_logits = lax.psum(jnp.dot(x_recv, w_router, preferred_element_type=jnp.float32), "section")
    own = lax.axis_index(EXPERT_AXES) // groups
    expert_ids = jnp.arange(experts, dtype=jnp.int32)[None, :]
    own_logit = jnp.sum(jnp.where(expert_ids == own, row_logits, zero_f), axis=1)
    other_logit = jnp.sum(jnp.where(expert_ids == other_recv[:, None], row_logits, zero_f), axis=1)
    row_gate = 1.0 / (1.0 + jnp.exp(other_logit - own_logit))
    gate_local = w_gate[0]
    up_local = w_up[0]
    down_local = w_down[0]
    pre_gate = jnp.dot(x_rows, gate_local, preferred_element_type=jnp.float32)
    pre_up = jnp.dot(x_rows, up_local, preferred_element_type=jnp.float32)
    sigmoid_gate = jax.nn.sigmoid(pre_gate)
    activated = pre_gate * sigmoid_gate
    hidden = (activated * pre_up).astype(jnp.bfloat16)
    hid = gate_local.shape[1]
    down_blocks = down_local.reshape(hid, n_section, width)
    gate_blocks = gate_local.reshape(n_section, width, hid)
    up_blocks = up_local.reshape(n_section, width, hid)
    out_piece = jnp.einsum("pf,fsd->spd", hidden, down_blocks, preferred_element_type=jnp.float32)
    out_piece = out_piece.astype(jnp.bfloat16).reshape(n_section * row_total, width)
    out_red = lax.psum_scatter(out_piece, "section", scatter_dimension=0, tiled=True)
    out_red, cot_recv, row_gate, gate_first, gate_second = lax.optimization_barrier(
        (out_red, cot_recv, row_gate, gate_first, gate_second)
    )
    cot_rows = lax.all_gather(cot_recv, "section", axis=1, tiled=True)
    dy_rows = (row_gate[:, None] * cot_rows.astype(jnp.float32)).astype(jnp.bfloat16)
    n_dev = row_total // capacity
    out_back = lax.all_to_all(out_red.reshape(n_dev, half, LANES), EXPERT_AXES, 0, 0, tiled=True)
    out_back = out_back.reshape(experts, groups, half, LANES).astype(jnp.float32)
    slot_out = jnp.sum(out_back, axis=1).reshape(slot_total, width)
    d_hidden = jnp.einsum("pd,fd->pf", dy_rows, down_local, preferred_element_type=jnp.float32)
    grad_down = jnp.einsum("pf,pd->fd", hidden, dy_rows, preferred_element_type=jnp.float32).astype(
        jnp.bfloat16
    )
    d_pre_gate = (
        d_hidden * pre_up * sigmoid_gate * (1.0 + pre_gate * (1.0 - sigmoid_gate))
    ).astype(jnp.bfloat16)
    d_pre_up = (d_hidden * activated).astype(jnp.bfloat16)
    grad_gate = jnp.einsum(
        "pd,pf->df", x_rows, d_pre_gate, preferred_element_type=jnp.float32
    ).astype(jnp.bfloat16)
    grad_up = jnp.einsum("pd,pf->df", x_rows, d_pre_up, preferred_element_type=jnp.float32).astype(
        jnp.bfloat16
    )
    first_float = pick_first.astype(jnp.float32)
    second_float = pick_second.astype(jnp.float32)
    out_first = jnp.dot(first_float, slot_out, precision=highest)
    out_second = jnp.dot(second_float, slot_out, precision=highest)
    mixed = (gate_first[:, None] * out_first + gate_second[:, None] * out_second).astype(
        jnp.bfloat16
    )
    local_inner = jnp.stack(
        [jnp.sum(cot_float * out_first, axis=1), jnp.sum(cot_float * out_second, axis=1)], axis=1
    )
    dx_piece = jnp.einsum(
        "pf,sdf->spd", d_pre_gate, gate_blocks, preferred_element_type=jnp.float32
    )
    dx_piece = dx_piece + jnp.einsum(
        "pf,sdf->spd", d_pre_up, up_blocks, preferred_element_type=jnp.float32
    )
    gate_inner = lax.psum(local_inner, "section")
    d_first = gate_first * gate_second * (gate_inner[:, 0] - gate_inner[:, 1])
    d_logits = jnp.where(route_hot[:, 0, :], d_first[:, None], zero_f) - jnp.where(
        route_hot[:, 1, :], d_first[:, None], zero_f
    )
    dx_piece = dx_piece.astype(jnp.bfloat16).reshape(n_section * row_total, width)
    d_logits, dx_piece = lax.optimization_barrier((d_logits, dx_piece))
    dx_red = lax.psum_scatter(dx_piece, "section", scatter_dimension=0, tiled=True)
    router_part = jnp.einsum("te,tf->ef", d_logits, tokens.astype(jnp.float32), precision=highest)
    router_part = lax.psum(router_part, EXPERT_AXES[2])
    for name in (EXPERT_AXES[1], EXPERT_AXES[0]):
        router_part = jnp.sum(lax.all_gather(router_part, name, axis=0), axis=0)
    router_part, dx_red = lax.optimization_barrier((router_part, dx_red))
    dx_back = lax.all_to_all(dx_red.reshape(n_dev, half, LANES), EXPERT_AXES, 0, 0, tiled=True)
    dx_back = dx_back.reshape(experts, groups, half, LANES).astype(jnp.float32)
    slot_dx = jnp.sum(dx_back, axis=1).reshape(slot_total, width)
    dx_expert = jnp.dot(first_float, slot_dx, precision=highest)
    dx_expert = dx_expert + jnp.dot(second_float, slot_dx, precision=highest)
    router_float = w_router.astype(jnp.float32)
    grad_tokens = (dx_expert + jnp.dot(d_logits, router_float.T, precision=highest)).astype(
        jnp.bfloat16
    )
    grad_router = router_part.T
    return (mixed, grad_tokens, grad_router, grad_gate[None], grad_up[None], grad_down[None])


def expert_shape(devices):
    try:
        xs = sorted({d.coords[0] for d in devices.flat})
        zs = sorted({d.coords[2] for d in devices.flat})
        cores = sorted({d.core_on_chip for d in devices.flat})
        shape = (len(xs), len(zs), len(cores))
    except AttributeError:
        shape = (4, 8, 2)
    if int(np.prod(shape)) != devices.shape[1]:
        shape = (devices.shape[1] // 16, 8, 2)
    return shape


def solution(mesh):
    devices = mesh.devices
    fine = Mesh(
        devices.reshape((devices.shape[0],) + expert_shape(devices)), ("section",) + EXPERT_AXES
    )
    ex = EXPERT_AXES
    in_specs = (
        P(ex, "section"),
        P(ex, "section"),
        P(ex, None),
        P("section", None),
        P(ex, None, "section"),
        P(ex, None, "section"),
        P(ex, "section", None),
    )
    out_specs = (
        P(ex, "section"),
        P(ex, "section"),
        P("section", None),
        P(ex, None, "section"),
        P(ex, None, "section"),
        P(ex, "section", None),
    )
    return jax.shard_map(
        per_device, mesh=fine, in_specs=in_specs, out_specs=out_specs, check_vma=False
    )
```

profile of v0, /device:TPU:1, one launch (start us, length us, event | category | flops | bytes accessed | tf_op | source)
XLA Modules:
  0.0 275.1 jit_solution(3696435519088308416)
XLA Ops:
  7.2 0.0 all-gather.4.cloned.1.call-start
  7.2 0.9 copy.41
  8.1 0.1 eq.76
  8.2 0.1 fusion.21
  8.3 0.1 reduce_window_sum.11
  8.3 0.2 select_reduce_fusion
  8.5 0.1 reshape.135
  8.6 0.1 copy.42
  8.7 0.7 multiply_add_fusion
  9.4 0.8 slice_bitcast_fusion.3
  10.2 1.0 convolution_convert_fusion.5
  11.2 0.1 broadcast_in_dim.97
  11.3 0.1 broadcast_in_dim.98
  11.4 35.8 %all_to_all.20 = bf16[64,48,128]{2,1,0:T(8,128)(2,1)S(1)} all-to-all(bf16[64,48,128]{2,1,0:T(8,128)(2,1)S(1)} %bitcast.102), channel_id=1, replica_groups=mesh['section'=4,'ex'=4,'ez'=8,'ec'=2] {'ex','ez','ec'}, dimensions={0} | all-to-all | bytes 1572864 | tf_op jit(solution)/shard_map/all_to_all | solution.py:58
  47.1 1.2 reshape.137
  48.4 0.0 reduce-scatter.3.cloned.1.call-start
  48.4 4.5 %reshape_squeeze.9 = bf16[256,4,1024]{2,1,0:T(4,128)(2,1)} reshape(bf16[1,256,4096]{2,1,0:T(8,128)(2,1)} %param.15) | data formatting | bytes 4194304 | tf_op jit(solution)/shard_map/reshape;squeeze | solution.py:92
  52.9 34.7 %all-gather.4.cloned.1.call-done = bf16[384,4096]{1,0:T(8,128)(2,1)} async-done(((bf16[384,1024]{1,0:T(8,128)(2,1)}), bf16[384,4096]{1,0:T(8,128)(2,1)}) %all-gather.4.cloned.1.call-update) | async-done | bytes 3145744 | tf_op jit(solution)/shard_map/all_gather | solution.py:65
  87.6 3.7 %fusion.7 = f32[384,256]{1,0:T(8,128)S(1)} fusion(bf16[384,4096]{1,0:T(8,128)(2,1)} %all-gather.4.cloned.1.call-done, bf16[1,4096,256]{2,1,0:T(8,128)(2,1)} %param.13), kind=kOutput, calls=%fused_computation.13 | convolution fusion | flops 805306368 | bytes 5636096 | tf_op jit(solution)/shard_map/dot_general | solution.py:86
  91.3 1.7 multiply_convert_fusion.5
  93.1 3.4 %convolution_convert_fusion.3 = bf16[384,4,1024]{2,0,1:T(8,128)(2,1)} fusion(bf16[256,4,1024]{2,1,0:T(4,128)(2,1)S(1)} %copy-done.1, bf16[384,256]{1,0:T(8,128)(2,1)S(1)} %get-tuple-element.59), kind=kOutput, calls=%fused_computation.8 | convolution fusion | flops 806879232 | bytes 5439488 | tf_op jit(solution)/shard_map/pf,fsd->spd/dot_general | solution.py:95
  96.5 0.1 add_reduce_fusion
  96.6 0.1 convert_element_type.122
  96.7 0.3 convolution_convert_fusion.4
  97.0 0.1 reshape.139
  97.1 1.2 broadcast_in_dim.104
  98.3 10.9 %all-to-all-start.1 = ((bf16[64,64,128]{2,1,0:T(8,128)(2,1)}), bf16[64,64,128]{2,1,0:T(8,128)(2,1)}, u32[]{:S(2)}, u32[]{:S(2)}) async-start(bf16[64,64,128]{2,1,0:T(8,128)(2,1)} %bitcast.101), calls=%async_computation.2 | async-start | bytes 2097152 | tf_op jit(solution)/shard_map/all_to_all | solution.py:67
  109.2 0.0 all-gather.6.cloned.1.call-start
  109.3 0.1 convolution_bitcast_fusion.1
  109.5 0.3 fusion.36
  109.8 13.5 %all-reduce.1 = (f32[384,8]{0,1:T(8,128)S(1)}, f32[16,8]{0,1:T(8,128)S(1)}) all-reduce(f32[384,8]{0,1:T(8,128)S(1)} %fusion.36, f32[16,8]{0,1:T(8,128)S(1)} %convolution_bitcast_fusion.1), channel_id=1, replica_groups=mesh['section'=4,'ex'=4,'ez'=8,'ec'=2] {'section'}, use_global_device_ids=true, to_apply=%region_4.5 | all-reduce | flops 3200 | bytes 25600 | tf_op jit(solution)/shard_map/psum | solution.py:77
  123.3 14.4 %all-to-all-done.1 = bf16[64,64,128]{2,1,0:T(8,128)(2,1)} async-done(((bf16[64,64,128]{2,1,0:T(8,128)(2,1)}), bf16[64,64,128]{2,1,0:T(8,128)(2,1)}, u32[]{:S(2)}, u32[]{:S(2)}) %all-to-all-start.1) | async-done | bytes 1048608 | tf_op jit(solution)/shard_map/all_to_all | solution.py:67
  137.7 1.0 fusion.20
  138.7 0.1 reshape.147
  138.9 1.2 slice.73
  140.1 1.2 reshape.141
  141.3 0.1 select_reduce_fusion.1
  141.4 2.2 reshape.142
  143.6 7.4 %all-to-all-start.2 = ((bf16[64,48,128]{2,1,0:T(8,128)(2,1)}), bf16[64,48,128]{2,1,0:T(8,128)(2,1)S(1)}, u32[]{:S(2)}, u32[]{:S(2)}) async-start(bf16[64,48,128]{2,1,0:T(8,128)(2,1)} %reshape.142), calls=%async_computation.3 | async-start | bytes 1572864 | tf_op jit(solution)/shard_map/all_to_all | solution.py:104
  151.0 0.0 reduce-scatter.5.cloned.1.call-start
  151.0 22.9 %all-to-all-done.2 = bf16[64,48,128]{2,1,0:T(8,128)(2,1)S(1)} async-done(((bf16[64,48,128]{2,1,0:T(8,128)(2,1)}), bf16[64,48,128]{2,1,0:T(8,128)(2,1)S(1)}, u32[]{:S(2)}, u32[]{:S(2)}) %all-to-all-start.2) | async-done | bytes 786464 | tf_op jit(solution)/shard_map/all_to_all | solution.py:104
  173.9 0.1 convert_reduce_fusion.1
  174.1 0.2 fusion.22
  174.3 1.0 fusion.18
  175.3 7.1 %psum.30 = f32[16,2]{0,1:T(2,128)S(1)} all-reduce(f32[16,2]{0,1:T(2,128)S(1)} %pad_maximum_fusion), channel_id=1, replica_groups=mesh['section'=4,'ex'=4,'ez'=8,'ec'=2] {'section'}, use_global_device_ids=true, to_apply=%region_12.13 | all-reduce | flops 32 | bytes 256 | tf_op jit(solution)/shard_map/psum | solution.py:137
  182.5 3.9 %multiply_convert_fusion.3 = (bf16[384,256]{1,0:T(8,128)(2,1)S(1)}, bf16[384,256]{1,0:T(8,128)(2,1)S(1)}) fusion(f32[384,256]{1,0:T(8,128)} %copy-done.10, f32[384,256]{1,0:T(8,128)} %get-tuple-element.60, bf16[1,256,4096]{2,1,0:T(8,128)(2,1)} %param.15, bf16[384,4096]{1,0:T(8,128)(2,1)} %all-gather.6.cloned.1.call-done, f32[384]{0:T(512)S(1)} %add_divide_fusion.1), kind=kOutput, calls=%fused_computation.25 | convolution fusion | flops 811302912 | bytes 6424064 | tf_op jit(solution)/shard_map/pd,fd->pf/dot_general | solution.py:107
  186.4 1.0 fusion.14
  187.4 2.9 %add_convert_fusion = bf16[384,4,1024]{2,0,1:T(8,128)(2,1)} fusion(f32[384,4,1024]{2,0,1:T(8,128)S(1)} %fusion.14, bf16[4,1024,256]{2,1,0:T(8,128)(2,1)S(1)} %bitcast.98, bf16[384,256]{1,0:T(8,128)(2,1)S(1)} %get-tuple-element.50), kind=kOutput, calls=%fused_computation | convolution fusion | flops 808452096 | bytes 11730944 | tf_op jit(solution)/shard_map/pf,sdf->spd/dot_general | solution.py:134
  190.3 0.1 convolution_bitcast_fusion
  190.4 5.2 %psum.31 = f32[1,8,1024]{2,1,0:T(8,128)S(1)} all-reduce(f32[1,8,1024]{2,1,0:T(8,128)S(1)} %convolution_bitcast_fusion), channel_id=1, replica_groups=mesh['section'=4,'ex'=4,'ez'=8,'ec'=2] {'ec'}, use_global_device_ids=true, to_apply=%region_13.14 | all-reduce | flops 8192 | bytes 65536 | tf_op jit(solution)/shard_map/psum | solution.py:146
  195.7 20.2 %all_gather.21 = f32[8,8,1024]{2,1,0:T(8,128)S(1)} all-gather(f32[1,8,1024]{2,1,0:T(8,128)S(1)} %psum.31), channel_id=1, replica_groups=mesh['section'=4,'ex'=4,'ez'=8,'ec'=2] {'ez'}, dimensions={0}, use_global_device_ids=true | all-gather | bytes 294912 | tf_op jit(solution)/shard_map/all_gather | solution.py:148
  215.8 10.6 %all-gather = f32[32,1024]{1,0:T(8,128)S(1)} all-gather(f32[8,1024]{1,0:T(8,128)S(1)} %reduce_sum.107), channel_id=2, replica_groups=mesh['section'=4,'ex'=4,'ez'=8,'ec'=2] {'ex'}, dimensions={0}, use_global_device_ids=true | all-gather | bytes 163840 | tf_op jit(solution)/shard_map/all_gather | solution.py:148
  226.5 0.6 bitcast_reduce_fusion
  227.1 4.2 %reduce-scatter.5.cloned.1.call-done = bf16[384,1024]{1,0:T(8,128)(2,1)} async-done(((bf16[1536,1024]{1,0:T(8,128)(2,1)}), bf16[384,1024]{1,0:T(8,128)(2,1)}) %reduce-scatter.5.cloned.1.call-update) | async-done | bytes 786448 | tf_op jit(solution)/shard_map/reduce_scatter | solution.py:144
  231.3 2.2 reshape.145
  233.5 10.6 %all-to-all-start.3 = ((bf16[64,48,128]{2,1,0:T(8,128)(2,1)}), bf16[64,48,128]{2,1,0:T(8,128)(2,1)S(1)}, u32[]{:S(2)}, u32[]{:S(2)}) async-start(bf16[64,48,128]{2,1,0:T(8,128)(2,1)} %reshape.145), calls=%async_computation.5 | async-start | bytes 1572864 | tf_op jit(solution)/shard_map/all_to_all | solution.py:150
  244.1 4.7 %fusion.2 = bf16[1,256,4096]{2,1,0:T(8,128)(2,1)} fusion(bf16[384,256]{1,0:T(8,128)(2,1)S(1)} %get-tuple-element.59, bf16[384,4096]{1,0:T(8,128)(2,1)} %all-gather.6.cloned.1.call-done, f32[384]{0:T(512)S(1)} %add_divide_fusion.1), kind=kOutput, calls=%fused_computation.7 | convolution fusion | flops 811073536 | bytes 5441024 | tf_op jit(solution)/shard_map/pf,pd->fd/dot_general | solution.py:108
  248.8 2.6 fusion
  251.4 2.6 fusion.1
  254.1 13.0 %all-to-all-done.3 = bf16[64,48,128]{2,1,0:T(8,128)(2,1)S(1)} async-done(((bf16[64,48,128]{2,1,0:T(8,128)(2,1)}), bf16[64,48,128]{2,1,0:T(8,128)(2,1)S(1)}, u32[]{:S(2)}, u32[]{:S(2)}) %all-to-all-start.3) | async-done | bytes 786464 | tf_op jit(solution)/shard_map/all_to_all | solution.py:150
  267.1 0.1 convert_reduce_fusion
  267.2 0.2 fusion.24
  267.5 0.2 convolution_add_fusion.1
  267.7 0.8 fusion.10
  (41 shorter events, 0.3 us)
Async XLA Ops:
  7.2 84.1 %copy-start = (bf16[1,4096,256]{2,1,0:T(8,128)(2,1)S(1)}, bf16[1,4096,256]{2,1,0:T(8,128)(2,1)}, u32[]{:S(2)}) copy-start(bf16[1,4096,256]{2,1,0:T(8,128)(2,1)} %param.14) | copy-start | bytes 6291460
  7.2 80.4 %all-gather.4.cloned.1.call-start = ((), (), s32[]{:S(2)}) async-start(), calls=%async_computation.6 | async-start | bytes 3932160 | tf_op jit(solution)/shard_map/all_gather | solution.py:65
  48.4 93.0 %reduce-scatter.3.cloned.1.call-start = ((), (), s32[]{:S(2)}) async-start(), calls=%async_computation.7 | async-start | bytes 3932160 | tf_op jit(solution)/shard_map/reduce_scatter | solution.py:97
  87.6 3.7 %copy-start.8 = (bf16[384,4096]{1,0:T(8,128)(2,1)S(1)}, bf16[384,4096]{1,0:T(8,128)(2,1)}, u32[]{:S(2)}) copy-start(bf16[384,4096]{1,0:T(8,128)(2,1)} %all-gather.4.cloned.1.call-done) | copy-start | bytes 9437188
  91.3 1.8 copy-start.10
  91.3 1.8 copy-start.1
  93.1 3.6 %copy-start.6 = (bf16[16,1024]{1,0:T(8,128)(2,1)S(1)}, bf16[16,1024]{1,0:T(8,128)(2,1)}, u32[]{:S(2)}) copy-start(bf16[16,1024]{1,0:T(8,128)(2,1)} %param.10) | copy-start | bytes 98308
  96.5 12.8 %copy-start.4 = (bf16[16,1024]{1,0:T(8,128)(2,1)S(1)}, bf16[16,1024]{1,0:T(8,128)(2,1)}, u32[]{:S(2)}) copy-start(bf16[16,1024]{1,0:T(8,128)(2,1)} %param.9) | copy-start | bytes 98308
  96.5 12.8 %copy-start.5 = (bf16[1024,8]{0,1:T(8,128)(2,1)S(1)}, bf16[1024,8]{0,1:T(8,128)(2,1)}, u32[]{:S(2)}) copy-start(bf16[1024,8]{0,1:T(8,128)(2,1)} %param.12) | copy-start | bytes 49156
  96.5 13.0 %copy-start.2 = (bf16[384,1024]{1,0:T(8,128)(2,1)S(1)}, bf16[384,1024]{1,0:T(8,128)(2,1)}, u32[]{:S(2)}) copy-start(bf16[384,1024]{1,0:T(8,128)(2,1)} %reshape.137) | copy-start | bytes 2359300
  96.5 26.8 %copy-start.7 = (s32[16,2]{0,1:T(2,128)S(1)}, s32[16,2]{0,1:T(2,128)}, u32[]{:S(2)}) copy-start(s32[16,2]{0,1:T(2,128)} %param.11) | copy-start | bytes 388
  98.3 39.4 %all-to-all-start.1 = ((bf16[64,64,128]{2,1,0:T(8,128)(2,1)}), bf16[64,64,128]{2,1,0:T(8,128)(2,1)}, u32[]{:S(2)}, u32[]{:S(2)}) async-start(bf16[64,64,128]{2,1,0:T(8,128)(2,1)} %bitcast.101), calls=%async_computation.2 | async-start | bytes 2097152 | tf_op jit(solution)/shard_map/all_to_all | solution.py:67
  109.2 73.2 %all-gather.6.cloned.1.call-start = ((), (), s32[]{:S(2)}) async-start(), calls=%async_computation.8 | async-start | bytes 3932160 | tf_op jit(solution)/shard_map/all_gather | solution.py:101
  143.6 30.4 %all-to-all-start.2 = ((bf16[64,48,128]{2,1,0:T(8,128)(2,1)}), bf16[64,48,128]{2,1,0:T(8,128)(2,1)S(1)}, u32[]{:S(2)}, u32[]{:S(2)}) async-start(bf16[64,48,128]{2,1,0:T(8,128)(2,1)} %reshape.142), calls=%async_computation.3 | async-start | bytes 1572864 | tf_op jit(solution)/shard_map/all_to_all | solution.py:104
  151.0 80.4 %reduce-scatter.5.cloned.1.call-start = ((), (), s32[]{:S(2)}) async-start(), calls=%async_computation.9 | async-start | bytes 3932160 | tf_op jit(solution)/shard_map/reduce_scatter | solution.py:144
  182.5 3.9 %copy-start.3 = (bf16[1,4096,256]{2,1,0:T(8,128)(2,1)S(1)}, bf16[1,4096,256]{2,1,0:T(8,128)(2,1)}, u32[]{:S(2)}) copy-start(bf16[1,4096,256]{2,1,0:T(8,128)(2,1)} %param.13) | copy-start | bytes 6291460
  233.5 33.6 %all-to-all-start.3 = ((bf16[64,48,128]{2,1,0:T(8,128)(2,1)}), bf16[64,48,128]{2,1,0:T(8,128)(2,1)S(1)}, u32[]{:S(2)}, u32[]{:S(2)}) async-start(bf16[64,48,128]{2,1,0:T(8,128)(2,1)} %reshape.145), calls=%async_computation.5 | async-start | bytes 1572864 | tf_op jit(solution)/shard_map/all_to_all | solution.py:150
  244.1 4.7 %copy-start.9 = (bf16[384,4096]{1,0:T(8,128)(2,1)S(1)}, bf16[384,4096]{1,0:T(8,128)(2,1)}, u32[]{:S(2)}) copy-start(bf16[384,4096]{1,0:T(8,128)(2,1)} %all-gather.4.cloned.1.call-done) | copy-start | bytes 9437188
Sparse Core Ops, SparseCore 0:
  48.5 39.0 all-gather.3
  96.6 41.3 reduce-scatter.2
  141.5 40.6 all-gather.5
  190.4 40.8 reduce-scatter.4
where the time goes:
time: 276 us; the launch traced here: 275 us
  blocking collectives  92.4 us (33%)
  waiting for transfers between devices  89.4 us (32%)
  matrix products  30.9 us (11%)
  starting transfers between devices  29.1 us (11%)
  local copies, waits for them, and re-layouts  16.1 us (6%)
  between operations  14.1 us (5%)
  other arithmetic  3.15 us (1%)
    all_to_all x1, blocking collectives, per_device(): x_recv = lax.all_to_all(spread(x_block), EXPERT_AXES, 0, 0, tiled=True)  35.8 us
    all_gather x1, waiting for transfers between devices, per_device(): x_rows = lax.all_gather(x_recv, 'section', axis=1, tiled=True)  34.7 us
    all_gather x2, blocking collectives, per_device(): router_part = jnp.sum(lax.all_gather(router_part, name, axis=0), axis=0)  30.8 us
    all_to_all x1, waiting for transfers between devices, per_device(): lax.all_to_all(out_red.reshape(n_dev, half, LANES), EXPERT_AXES, 0, 0, ti...  22.9 us
    all_to_all x1, waiting for transfers between devices, per_device(): c_recv = lax.all_to_all(spread(c_block), EXPERT_AXES, 0, 0, tiled=True)  14.4 us
    psum x1, blocking collectives, per_device(): lax.psum(jnp.dot(x_recv, w_router, preferred_element_type=jnp.float32), '...  13.5 us
    all_to_all x1, waiting for transfers between devices, per_device(): lax.all_to_all(dx_red.reshape(n_dev, half, LANES), EXPERT_AXES, 0, 0, til...  13 us
    all_to_all x1, starting transfers between devices, per_device(): c_recv = lax.all_to_all(spread(c_block), EXPERT_AXES, 0, 0, tiled=True)  10.9 us
  transfers between devices with their start and end apart: 7, of which 5 were waited for; matrix products, arithmetic and copies ran while one was open for 9% of the time, Pallas kernels for 0%

commit v1 on v0

--- a/solution.py
+++ b/solution.py
@@ -62,7 +62,14 @@
     c_block = jnp.concatenate([cot_source.reshape(experts, half, LANES), meta], axis=1)
     row_total = x_recv.shape[0] * capacity
     x_recv = x_recv.reshape(row_total, width)
-    x_rows = lax.all_gather(x_recv, "section", axis=1, tiled=True)
+    ring = [x_recv]
+    for hop in range(3):
+        ring.append(lax.ppermute(ring[-1], "section", [(dev, (dev + 1) % 4) for dev in range(4)]))
+    x_rows = jnp.roll(
+        jnp.concatenate(ring[::-1], axis=1),
+        (lax.axis_index("section") + 1) * ring[0].shape[1],
+        axis=1,
+    )
     c_block, x_recv = lax.optimization_barrier((c_block, x_recv))
     c_recv = lax.all_to_all(spread(c_block), EXPERT_AXES, 0, 0, tiled=True)
     cot_recv = c_recv[:, :half].reshape(row_total, width)

time: 276 us -> 297 us (1.076)
  waiting for transfers between devices: 89.4 us -> 105 us
  local copies, waits for them, and re-layouts: 16.1 us -> 23.6 us
    ppermute x0 -> x3, waiting for transfers between devices: none -> 52 us  [per_device(): lax.ppermute(ring[-1], 'section', [(dev, (dev + 1) % 4) for dev in range(...]
    all_gather x1 -> x0, waiting for transfers between devices: 34.7 us -> none  [per_device(): x_rows = lax.all_gather(x_recv, 'section', axis=1, tiled=True)]
    unnamed x23 -> x34, local copies, waits for them, and re-layouts: 0.95 us -> 8.18 us
  transfers between devices with their start and end apart: 7 -> 9, of which waited for: 5 -> 7; matrix products, arithmetic and copies ran while one was open for 9% -> 9% of each run, Pallas kernels for 0% -> 0%
where the time goes in v1:
time: 297 us; the launch traced here: 296 us
  waiting for transfers between devices  105 us (35%)
  blocking collectives  92 us (31%)
  matrix products  30.1 us (10%)
  starting transfers between devices  27.9 us (9%)
  local copies, waits for them, and re-layouts  23.6 us (8%)
  between operations  14.1 us (5%)
  other arithmetic  3.15 us (1%)
    ppermute x3, waiting for transfers between devices, per_device(): lax.ppermute(ring[-1], 'section', [(dev, (dev + 1) % 4) for dev in range(...  52 us
    all_to_all x1, blocking collectives, per_device(): x_recv = lax.all_to_all(spread(x_block), EXPERT_AXES, 0, 0, tiled=True)  35.9 us
    all_gather x2, blocking collectives, per_device(): router_part = jnp.sum(lax.all_gather(router_part, name, axis=0), axis=0)  31 us
    all_to_all x1, waiting for transfers between devices, per_device(): lax.all_to_all(out_red.reshape(n_dev, half, LANES), EXPERT_AXES, 0, 0, ti...  22.9 us
    all_to_all x1, waiting for transfers between devices, per_device(): c_recv = lax.all_to_all(spread(c_block), EXPERT_AXES, 0, 0, tiled=True)  14.8 us
    psum x1, blocking collectives, per_device(): lax.psum(jnp.dot(x_recv, w_router, preferred_element_type=jnp.float32), '...  13.1 us
    all_to_all x1, waiting for transfers between devices, per_device(): lax.all_to_all(dx_red.reshape(n_dev, half, LANES), EXPERT_AXES, 0, 0, til...  11.1 us
    all_to_all x1, starting transfers between devices, per_device(): lax.all_to_all(dx_red.reshape(n_dev, half, LANES), EXPERT_AXES, 0, 0, til...  10.6 us
  transfers between devices with their start and end apart: 9, of which 7 were waited for; matrix products, arithmetic and copies ran while one was open for 9% of the time, Pallas kernels for 0%

profile of v1, /device:TPU:1, one launch (start us, length us, event | category | flops | bytes accessed | tf_op | source)
XLA Modules:
  0.0 296.1 jit_solution(17639754391339470567)
XLA Ops:
  7.2 0.9 copy.41
  8.1 0.1 eq.79
  8.3 0.2 select_reduce_fusion
  8.6 0.1 copy.42
  8.7 0.7 multiply_add_fusion
  9.4 0.8 slice_bitcast_fusion.3
  10.2 1.0 convolution_convert_fusion.5
  11.3 0.1 broadcast_in_dim.98
  11.4 35.9 %all_to_all.20 = bf16[64,48,128]{2,1,0:T(8,128)(2,1)} all-to-all(bf16[64,48,128]{2,1,0:T(8,128)(2,1)S(1)} %bitcast.98), channel_id=1, replica_groups=mesh['section'=4,'ex'=4,'ez'=8,'ec'=2] {'ex','ez','ec'}, dimensions={0} | all-to-all | bytes 1572864 | tf_op jit(solution)/shard_map/all_to_all | solution.py:58
  47.2 1.4 reshape.137
  48.7 1.4 collective-permute-start
  50.0 18.8 %collective-permute-done = bf16[384,1024]{1,0:T(8,128)(2,1)S(1)} collective-permute-done((bf16[384,1024]{1,0:T(8,128)(2,1)S(1)}, bf16[384,1024]{1,0:T(8,128)(2,1)S(1)}, u32[]{:S(2)}, u32[]{:S(2)}) %collective-permute-start) | collective-permute-done | bytes 786464 | tf_op jit(solution)/shard_map/ppermute | solution.py:67
  68.8 0.9 copy-done.3
  69.7 19.2 %collective-permute-done.1 = bf16[384,1024]{1,0:T(8,128)(2,1)} collective-permute-done((bf16[384,1024]{1,0:T(8,128)(2,1)S(1)}, bf16[384,1024]{1,0:T(8,128)(2,1)}, u32[]{:S(2)}, u32[]{:S(2)}) %collective-permute-start.1) | collective-permute-done | bytes 786464 | tf_op jit(solution)/shard_map/ppermute | solution.py:67
  88.9 4.5 %reshape_squeeze.9 = bf16[256,4,1024]{2,1,0:T(4,128)(2,1)} reshape(bf16[1,256,4096]{2,1,0:T(8,128)(2,1)} %param.15) | data formatting | bytes 4194304 | tf_op jit(solution)/shard_map/reshape;squeeze | solution.py:99
  93.4 14.0 %collective-permute-done.2 = bf16[384,1024]{1,0:T(8,128)(2,1)} collective-permute-done((bf16[384,1024]{1,0:T(8,128)(2,1)}, bf16[384,1024]{1,0:T(8,128)(2,1)}, u32[]{:S(2)}, u32[]{:S(2)}) %collective-permute-start.2) | collective-permute-done | bytes 786464 | tf_op jit(solution)/shard_map/ppermute | solution.py:67
  107.4 1.2 constant_dynamic-update-slice_fusion.7
  108.6 1.2 constant_dynamic-update-slice_fusion.6
  109.9 1.3 constant_dynamic-update-slice_fusion.3
  111.3 1.2 constant_dynamic-update-slice_fusion.2
  112.6 1.0 fusion.7
  113.7 1.7 multiply_convert_fusion.5
  115.5 0.2 copy-done.12
  115.7 1.0 copy-done.1
  116.7 3.4 %convolution_convert_fusion.3 = bf16[384,4,1024]{2,0,1:T(8,128)(2,1)} fusion(bf16[256,4,1024]{2,1,0:T(4,128)(2,1)S(1)} %copy-done.1, bf16[384,256]{1,0:T(8,128)(2,1)S(1)} %get-tuple-element.59), kind=kOutput, calls=%fused_computation.8 | convolution fusion | flops 806879232 | bytes 5439488 | tf_op jit(solution)/shard_map/pf,fsd->spd/dot_general | solution.py:102
  120.1 0.1 add_reduce_fusion
  120.2 0.1 convert_element_type.122
  120.3 0.3 convolution_convert_fusion.4
  120.7 1.2 broadcast_in_dim.104
  121.9 9.6 %all-to-all-start.1 = ((bf16[64,64,128]{2,1,0:T(8,128)(2,1)}), bf16[64,64,128]{2,1,0:T(8,128)(2,1)}, u32[]{:S(2)}, u32[]{:S(2)}) async-start(bf16[64,64,128]{2,1,0:T(8,128)(2,1)} %bitcast.97), calls=%async_computation.2 | async-start | bytes 2097152 | tf_op jit(solution)/shard_map/all_to_all | solution.py:74
  131.7 0.1 convolution_bitcast_fusion.1
  131.8 0.3 fusion.44
  132.1 13.1 %all-reduce.1 = (f32[384,8]{0,1:T(8,128)S(1)}, f32[16,8]{0,1:T(8,128)S(1)}) all-reduce(f32[384,8]{0,1:T(8,128)S(1)} %fusion.44, f32[16,8]{0,1:T(8,128)S(1)} %convolution_bitcast_fusion.1), channel_id=1, replica_groups=mesh['section'=4,'ex'=4,'ez'=8,'ec'=2] {'section'}, use_global_device_ids=true, to_apply=%region_4.5 | all-reduce | flops 3200 | bytes 25600 | tf_op jit(solution)/shard_map/psum | solution.py:84
  145.2 14.8 %all-to-all-done.1 = bf16[64,64,128]{2,1,0:T(8,128)(2,1)} async-done(((bf16[64,64,128]{2,1,0:T(8,128)(2,1)}), bf16[64,64,128]{2,1,0:T(8,128)(2,1)}, u32[]{:S(2)}, u32[]{:S(2)}) %all-to-all-start.1) | async-done | bytes 1048608 | tf_op jit(solution)/shard_map/all_to_all | solution.py:74
  160.0 1.0 fusion.24
  161.0 0.1 reshape.147
  161.2 1.2 slice.73
  162.4 1.2 reshape.141
  163.7 2.2 reshape.142
  165.9 6.2 %all-to-all-start.2 = ((bf16[64,48,128]{2,1,0:T(8,128)(2,1)}), bf16[64,48,128]{2,1,0:T(8,128)(2,1)S(1)}, u32[]{:S(2)}, u32[]{:S(2)}) async-start(bf16[64,48,128]{2,1,0:T(8,128)(2,1)} %reshape.142), calls=%async_computation.3 | async-start | bytes 1572864 | tf_op jit(solution)/shard_map/all_to_all | solution.py:111
  172.1 22.9 %all-to-all-done.2 = bf16[64,48,128]{2,1,0:T(8,128)(2,1)S(1)} async-done(((bf16[64,48,128]{2,1,0:T(8,128)(2,1)}), bf16[64,48,128]{2,1,0:T(8,128)(2,1)S(1)}, u32[]{:S(2)}, u32[]{:S(2)}) %all-to-all-start.2) | async-done | bytes 786464 | tf_op jit(solution)/shard_map/all_to_all | solution.py:111
  195.1 0.1 convert_reduce_fusion.1
  195.2 0.2 fusion.26
  195.4 1.0 fusion.22
  196.4 7.0 %psum.30 = f32[16,2]{0,1:T(2,128)S(1)} all-reduce(f32[16,2]{0,1:T(2,128)S(1)} %pad_maximum_fusion), channel_id=1, replica_groups=mesh['section'=4,'ex'=4,'ez'=8,'ec'=2] {'section'}, use_global_device_ids=true, to_apply=%region_12.13 | all-reduce | flops 32 | bytes 256 | tf_op jit(solution)/shard_map/psum | solution.py:144
  203.5 3.9 %multiply_convert_fusion.3 = (bf16[384,256]{1,0:T(8,128)(2,1)S(1)}, bf16[384,256]{1,0:T(8,128)(2,1)S(1)}) fusion(f32[384,256]{1,0:T(8,128)} %copy-done.12, f32[384,256]{1,0:T(8,128)} %get-tuple-element.60, bf16[1,256,4096]{2,1,0:T(8,128)(2,1)} %param.15, bf16[384,4096]{1,0:T(8,128)(2,1)} %all-gather.3.cloned.1.call-done, f32[384]{0:T(512)S(1)} %add_divide_fusion.1), kind=kOutput, calls=%fused_computation.29 | convolution fusion | flops 811302912 | bytes 6424064 | tf_op jit(solution)/shard_map/pd,fd->pf/dot_general | solution.py:114
  207.4 1.0 fusion.18
  208.4 2.8 add_convert_fusion
  211.3 0.1 convolution_bitcast_fusion
  211.4 5.0 %psum.31 = f32[1,8,1024]{2,1,0:T(8,128)S(1)} all-reduce(f32[1,8,1024]{2,1,0:T(8,128)S(1)} %convolution_bitcast_fusion), channel_id=1, replica_groups=mesh['section'=4,'ex'=4,'ez'=8,'ec'=2] {'ec'}, use_global_device_ids=true, to_apply=%region_13.14 | all-reduce | flops 8192 | bytes 65536 | tf_op jit(solution)/shard_map/psum | solution.py:153
  216.4 20.2 %all_gather.17 = f32[8,8,1024]{2,1,0:T(8,128)S(1)} all-gather(f32[1,8,1024]{2,1,0:T(8,128)S(1)} %psum.31), channel_id=1, replica_groups=mesh['section'=4,'ex'=4,'ez'=8,'ec'=2] {'ez'}, dimensions={0}, use_global_device_ids=true | all-gather | bytes 294912 | tf_op jit(solution)/shard_map/all_gather | solution.py:155
  236.7 10.8 %all-gather = f32[32,1024]{1,0:T(8,128)S(1)} all-gather(f32[8,1024]{1,0:T(8,128)S(1)} %reduce_sum.107), channel_id=2, replica_groups=mesh['section'=4,'ex'=4,'ez'=8,'ec'=2] {'ex'}, dimensions={0}, use_global_device_ids=true | all-gather | bytes 163840 | tf_op jit(solution)/shard_map/all_gather | solution.py:155
  247.4 0.6 bitcast_reduce_fusion
  248.1 4.2 %reduce-scatter.5.cloned.1.call-done = bf16[384,1024]{1,0:T(8,128)(2,1)} async-done(((bf16[1536,1024]{1,0:T(8,128)(2,1)}), bf16[384,1024]{1,0:T(8,128)(2,1)}) %reduce-scatter.5.cloned.1.call-update) | async-done | bytes 786448 | tf_op jit(solution)/shard_map/reduce_scatter | solution.py:151
  252.3 2.2 reshape.145
  254.5 10.6 %all-to-all-start.3 = ((bf16[64,48,128]{2,1,0:T(8,128)(2,1)}), bf16[64,48,128]{2,1,0:T(8,128)(2,1)S(1)}, u32[]{:S(2)}, u32[]{:S(2)}) async-start(bf16[64,48,128]{2,1,0:T(8,128)(2,1)} %reshape.145), calls=%async_computation.5 | async-start | bytes 1572864 | tf_op jit(solution)/shard_map/all_to_all | solution.py:157
  265.1 4.5 %fusion.1 = bf16[1,4096,256]{2,1,0:T(8,128)(2,1)} fusion(bf16[384,256]{1,0:T(8,128)(2,1)S(1)} %get-tuple-element.50, bf16[384,8192]{1,0:T(8,128)(2,1)} %copy-done.10, s32[]{:T(128)S(6)} %select_n.44), kind=kOutput, calls=%fused_computation.6 | convolution fusion | flops 806354944 | bytes 5439492 | tf_op jit(solution)/shard_map/pd,pf->df/dot_general | solution.py:125
  269.6 4.7 %fusion = bf16[1,4096,256]{2,1,0:T(8,128)(2,1)} fusion(bf16[384,256]{1,0:T(8,128)(2,1)S(1)} %get-tuple-element.51, bf16[384,8192]{1,0:T(8,128)(2,1)} %copy-done.10, s32[]{:T(128)S(6)} %select_n.44), kind=kOutput, calls=%fused_computation.5 | convolution fusion | flops 806354944 | bytes 5439492 | tf_op jit(solution)/shard_map/pd,pf->df/dot_general | solution.py:122
  274.3 2.7 fusion.2
  277.0 11.1 %all-to-all-done.3 = bf16[64,48,128]{2,1,0:T(8,128)(2,1)S(1)} async-done(((bf16[64,48,128]{2,1,0:T(8,128)(2,1)}), bf16[64,48,128]{2,1,0:T(8,128)(2,1)S(1)}, u32[]{:S(2)}, u32[]{:S(2)}) %all-to-all-start.3) | async-done | bytes 786464 | tf_op jit(solution)/shard_map/all_to_all | solution.py:157
  288.1 0.1 convert_reduce_fusion
  288.2 0.2 fusion.28
  288.4 0.2 convolution_add_fusion.1
  288.7 0.8 fusion.14
  (56 shorter events, 1.1 us)
Async XLA Ops:
  7.2 106.5 %copy-start = (bf16[1,4096,256]{2,1,0:T(8,128)(2,1)S(1)}, bf16[1,4096,256]{2,1,0:T(8,128)(2,1)}, u32[]{:S(2)}) copy-start(bf16[1,4096,256]{2,1,0:T(8,128)(2,1)} %param.14) | copy-start | bytes 6291460
  7.2 156.5 %reduce-scatter.3.cloned.1.call-start = ((), (), s32[]{:S(2)}) async-start(), calls=%async_computation.6 | async-start | bytes 3932160 | tf_op jit(solution)/shard_map/reduce_scatter | solution.py:104
  48.7 20.1 %collective-permute-start = (bf16[384,1024]{1,0:T(8,128)(2,1)S(1)}, bf16[384,1024]{1,0:T(8,128)(2,1)S(1)}, u32[]{:S(2)}, u32[]{:S(2)}) collective-permute-start(bf16[384,1024]{1,0:T(8,128)(2,1)S(1)} %reshape.137), channel_id=1, source_target_pairs={{0,64},{64,128},{128,192},{192,0},{1,65},{65,129},{129,193},{193,1... | collective-permute-start | bytes 2359304 | tf_op jit(solution)/shard_map/ppermute | solution.py:67
  68.8 0.9 copy-start.3
  69.7 19.2 %collective-permute-start.1 = (bf16[384,1024]{1,0:T(8,128)(2,1)S(1)}, bf16[384,1024]{1,0:T(8,128)(2,1)}, u32[]{:S(2)}, u32[]{:S(2)}) collective-permute-start(bf16[384,1024]{1,0:T(8,128)(2,1)S(1)} %collective-permute-done), channel_id=1, source_target_pairs={{0,64},{64,128},{128,192},{192,0},{1,65},{65,129},{129,193},{193,1... | collective-permute-start | bytes 2359304 | tf_op jit(solution)/shard_map/ppermute | solution.py:67
  88.9 18.5 %collective-permute-start.2 = (bf16[384,1024]{1,0:T(8,128)(2,1)}, bf16[384,1024]{1,0:T(8,128)(2,1)}, u32[]{:S(2)}, u32[]{:S(2)}) collective-permute-start(bf16[384,1024]{1,0:T(8,128)(2,1)} %collective-permute-done.1), channel_id=1, source_target_pairs={{0,64},{64,128},{128,192},{192,0},{1,65},{65,129},{129,193},{193,1... | collective-permute-start | bytes 2359304 | tf_op jit(solution)/shard_map/ppermute | solution.py:67
  93.4 16.4 %copy-start.4 = (bf16[384,1024]{1,0:T(8,128)(2,1)S(1)}, bf16[384,1024]{1,0:T(8,128)(2,1)}, u32[]{:S(2)}) copy-start(bf16[384,1024]{1,0:T(8,128)(2,1)} %copy-done.3) | copy-start | bytes 2359300
  109.9 2.7 copy-start.5
  112.6 2.8 copy-start.10
  113.7 2.0 copy-start.12
  113.7 3.0 %copy-start.1 = (bf16[256,4,1024]{2,1,0:T(4,128)(2,1)S(1)}, bf16[256,4,1024]{2,1,0:T(4,128)(2,1)}, u32[]{:S(2)}) copy-start(bf16[256,4,1024]{2,1,0:T(4,128)(2,1)} %reshape_squeeze.9) | copy-start | bytes 6291460
  116.7 3.6 %copy-start.9 = (bf16[16,1024]{1,0:T(8,128)(2,1)S(1)}, bf16[16,1024]{1,0:T(8,128)(2,1)}, u32[]{:S(2)}) copy-start(bf16[16,1024]{1,0:T(8,128)(2,1)} %param.10) | copy-start | bytes 98308
  120.1 11.6 %copy-start.7 = (bf16[16,1024]{1,0:T(8,128)(2,1)S(1)}, bf16[16,1024]{1,0:T(8,128)(2,1)}, u32[]{:S(2)}) copy-start(bf16[16,1024]{1,0:T(8,128)(2,1)} %param.9) | copy-start | bytes 98308
  120.1 11.6 %copy-start.8 = (bf16[1024,8]{0,1:T(8,128)(2,1)S(1)}, bf16[1024,8]{0,1:T(8,128)(2,1)}, u32[]{:S(2)}) copy-start(bf16[1024,8]{0,1:T(8,128)(2,1)} %param.12) | copy-start | bytes 49156
  120.1 25.0 %copy-start.11 = (s32[16,2]{0,1:T(2,128)S(1)}, s32[16,2]{0,1:T(2,128)}, u32[]{:S(2)}) copy-start(s32[16,2]{0,1:T(2,128)} %param.11) | copy-start | bytes 388
  121.9 38.1 %all-to-all-start.1 = ((bf16[64,64,128]{2,1,0:T(8,128)(2,1)}), bf16[64,64,128]{2,1,0:T(8,128)(2,1)}, u32[]{:S(2)}, u32[]{:S(2)}) async-start(bf16[64,64,128]{2,1,0:T(8,128)(2,1)} %bitcast.97), calls=%async_computation.2 | async-start | bytes 2097152 | tf_op jit(solution)/shard_map/all_to_all | solution.py:74
  131.6 71.9 %all-gather.3.cloned.1.call-start = ((), (), s32[]{:S(2)}) async-start(), calls=%async_computation.7 | async-start | bytes 3932160 | tf_op jit(solution)/shard_map/all_gather | solution.py:108
  165.9 29.2 %all-to-all-start.2 = ((bf16[64,48,128]{2,1,0:T(8,128)(2,1)}), bf16[64,48,128]{2,1,0:T(8,128)(2,1)S(1)}, u32[]{:S(2)}, u32[]{:S(2)}) async-start(bf16[64,48,128]{2,1,0:T(8,128)(2,1)} %reshape.142), calls=%async_computation.3 | async-start | bytes 1572864 | tf_op jit(solution)/shard_map/all_to_all | solution.py:111
  172.1 80.2 %reduce-scatter.5.cloned.1.call-start = ((), (), s32[]{:S(2)}) async-start(), calls=%async_computation.8 | async-start | bytes 3932160 | tf_op jit(solution)/shard_map/reduce_scatter | solution.py:151
  203.5 3.9 %copy-start.6 = (bf16[1,4096,256]{2,1,0:T(8,128)(2,1)S(1)}, bf16[1,4096,256]{2,1,0:T(8,128)(2,1)}, u32[]{:S(2)}) copy-start(bf16[1,4096,256]{2,1,0:T(8,128)(2,1)} %param.13) | copy-start | bytes 6291460
  254.5 33.6 %all-to-all-start.3 = ((bf16[64,48,128]{2,1,0:T(8,128)(2,1)}), bf16[64,48,128]{2,1,0:T(8,128)(2,1)S(1)}, u32[]{:S(2)}, u32[]{:S(2)}) async-start(bf16[64,48,128]{2,1,0:T(8,128)(2,1)} %reshape.145), calls=%async_computation.5 | async-start | bytes 1572864 | tf_op jit(solution)/shard_map/all_to_all | solution.py:157
  269.6 4.7 %copy-start.2 = (bf16[384,4096]{1,0:T(8,128)(2,1)S(1)}, bf16[384,4096]{1,0:T(8,128)(2,1)}, u32[]{:S(2)}) copy-start(bf16[384,4096]{1,0:T(8,128)(2,1)} %all-gather.3.cloned.1.call-done) | copy-start | bytes 9437188
Sparse Core Ops, SparseCore 0:
  120.2 39.0 reduce-scatter.2
  163.8 39.4 all-gather.2
  211.4 40.8 reduce-scatter.4
